TPU v7x, 512 devices: a whole 4x4x16 slice. The times are simulated.
512 devices in a mesh: expert: 32 (over x, y, core), replica: 16 (over z).
Axes of the slice: x: 4, y: 4, z: 16, core: 2. Of those that a mesh axis runs over, the one named last changes fastest.
Arguments:
- tokens: bfloat16 [65536, 2560], P(('expert', 'replica')), may hold values from -6 to 6
- cotangent: bfloat16 [65536, 2560], P(('expert', 'replica')), may hold values from -4 to 4
- partner: int32 [65536, 1], P(('expert', 'replica')), may hold values from 0 to 31; in each aligned block of 128 rows (0 to 127, 128 to 255, ...) at most 5 rows name the same one
- combine: int32 [65536, 2], P(('expert', 'replica')), may hold values from 1 to 8
- counts: int32 [512], P(('expert', 'replica')), may hold values from 32 to 128, as said below
- w_gate: bfloat16 [32, 2560, 768], P('expert', 'replica'), may hold values from -0.125 to 0.125
- w_up: bfloat16 [32, 2560, 768], P('expert', 'replica'), may hold values from -0.125 to 0.125
- w_down: bfloat16 [32, 768, 2560], P('expert', 'replica'), may hold values from -0.21875 to 0.21875
Outputs:
- token_grad: bfloat16 [65536, 2560], P(('expert', 'replica'))
- grad_down: bfloat16 [32, 768, 2560], P('expert', 'replica')
Inputs may be any that keep to these rules, and one draw needn't show every extreme that they name: `partner`: within the 128 rows of one device no expert index is named by more than 5 rows, and some device names one exactly 5 times. `counts`: some device has all 128 slots real.
All inputs are finite; a program needn't handle non-finite values.
Results may differ from a plain program's by a relative error of at most 0.017.
Values may be sent and summed in bfloat16 or wider, within the bound.
No kernel may reach another device: no remote copies, remote signals or barrier semaphores. Data moves between devices by JAX's collectives and lax.ppermute only.
A program may use at most 64 MiB of HBM per device.

v0:
```python
import jax
import jax.numpy as jnp
from jax import lax
from jax.sharding import PartitionSpec as P


def against_rows(left, matrix):
    return lax.dot_general(
        left, matrix, (((1,), (1,)), ((), ())), preferred_element_type=jnp.float32
    )


def expert_backward(inputs, upstream, gate_w, up_w, down_w):
    gate_act = jnp.dot(inputs, gate_w, preferred_element_type=jnp.float32)
    up_act = jnp.dot(inputs, up_w, preferred_element_type=jnp.float32)
    sigmoid_gate = jax.nn.sigmoid(gate_act)
    swish_gate = gate_act * sigmoid_gate
    hidden = (swish_gate * up_act).astype(jnp.bfloat16)
    hidden_grad = against_rows(upstream, down_w)
    gate_grad = (
        hidden_grad * up_act * sigmoid_gate * (1.0 + gate_act * (1.0 - sigmoid_gate))
    ).astype(jnp.bfloat16)
    up_grad = (hidden_grad * swish_gate).astype(jnp.bfloat16)
    input_grad = against_rows(gate_grad, gate_w) + against_rows(up_grad, up_w)
    return (hidden, input_grad)


def local(tokens, cotangent, partner, combine, counts, w_gate, w_up, w_down):
    tok_rows = tokens.shape[0]
    width = tokens.shape[1]
    expert_count = lax.axis_size("expert")
    capacity = max(2, (5 * tok_rows // 4 + expert_count - 1) // expert_count)
    positions = jnp.arange(tok_rows, dtype=jnp.int32)
    valid_rows = positions < counts[0]
    weights = combine.astype(jnp.float32)
    weight_sum = weights[:, 0] + weights[:, 1]
    share_home = jnp.where(valid_rows, weights[:, 0] / weight_sum, 0.0)
    share_away = jnp.where(valid_rows, weights[:, 1] / weight_sum, 0.0)
    upstream = cotangent.astype(jnp.float32)
    q_home = (upstream * share_home[:, None]).astype(jnp.bfloat16)
    q_away = (upstream * share_away[:, None]).astype(jnp.bfloat16)
    gate_full, up_full, down_full = (
        lax.all_gather(w_gate, "replica", axis=1, tiled=True),
        lax.all_gather(w_up, "replica", axis=1, tiled=True),
        lax.all_gather(w_down, "replica", axis=1, tiled=True),
    )
    gate_w = gate_full.reshape(gate_full.shape[1], gate_full.shape[2])
    up_w = up_full.reshape(up_full.shape[1], up_full.shape[2])
    down_w = down_full.reshape(down_full.shape[1], down_full.shape[2])
    target = partner[:, 0]
    onehot_rows = (target[:, None] == jnp.arange(expert_count, dtype=jnp.int32)[None, :]).astype(
        jnp.int32
    )
    rank_within = jnp.sum((jnp.cumsum(onehot_rows, axis=0) - onehot_rows) * onehot_rows, axis=1)
    destination = target * capacity + rank_within
    placing = (
        jnp.arange(expert_count * capacity, dtype=jnp.int32)[:, None] == destination[None, :]
    ).astype(jnp.bfloat16)
    send_x = (
        jnp.dot(placing, tokens, preferred_element_type=jnp.float32)
        .astype(jnp.bfloat16)
        .reshape(expert_count, capacity, width)
    )
    send_q = (
        jnp.dot(placing, q_away, preferred_element_type=jnp.float32)
        .astype(jnp.bfloat16)
        .reshape(expert_count, capacity, width)
    )
    hidden_home, grad_home = expert_backward(tokens, q_home, gate_w, up_w, down_w)
    x_there = lax.all_to_all(send_x, "expert", split_axis=0, concat_axis=0, tiled=True)
    q_there = lax.all_to_all(send_q, "expert", split_axis=0, concat_axis=0, tiled=True)
    item_count = x_there.shape[1]
    hidden_there, grad_there = expert_backward(
        x_there.reshape(-1, width), q_there.reshape(-1, width), gate_w, up_w, down_w
    )
    returned = lax.all_to_all(
        grad_there.astype(jnp.bfloat16).reshape(expert_count, item_count, width),
        "expert",
        split_axis=0,
        concat_axis=0,
        tiled=True,
    )
    returned, hidden_away, q_there = (
        returned,
        hidden_there.reshape(expert_count, item_count, -1),
        q_there,
    )
    contract = (((0,), (0,)), ((), ()))
    flat_returned = returned.reshape(expert_count * capacity, width)
    grad_away = lax.dot_general(
        placing, flat_returned, contract, preferred_element_type=jnp.float32
    )
    token_grad = (grad_home + grad_away).astype(jnp.bfloat16)
    flat_hidden = hidden_away.reshape(expert_count * capacity, -1)
    flat_q = q_there.reshape(expert_count * capacity, width)
    grad_down = lax.psum_scatter(
        (
            lax.dot_general(hidden_home, q_home, contract, preferred_element_type=jnp.float32)
            + lax.dot_general(flat_hidden, flat_q, contract, preferred_element_type=jnp.float32)
        ).astype(jnp.bfloat16),
        "replica",
        scatter_dimension=0,
        tiled=True,
    )
    return (token_grad, grad_down[None])


def solution(mesh):
    placed = (
        P(("expert", "replica"), None),
        P(("expert", "replica"), None),
        P(("expert", "replica"), None),
        P(("expert", "replica"), None),
        P(("expert", "replica")),
        P("expert", "replica", None),
        P("expert", "replica", None),
        P("expert", "replica", None),
    )
    return jax.shard_map(
        local,
        mesh=mesh,
        in_specs=placed,
        out_specs=(P(("expert", "replica"), None), P("expert", "replica", None)),
        check_vma=False,
    )
```

profile of v0, /device:TPU:10, one launch (start us, length us, event | category | flops | bytes accessed | tf_op | source)
XLA Modules:
  0.0 331.8 jit_solution(12413700207397267182)
XLA Ops:
  7.2 0.0 copy-start
  7.2 0.0 all-gather.8.cloned.1.call-start
  7.2 0.7 all-gather.8.cloned.1.call-update
  7.9 0.0 all-gather.6.cloned.1.call-start
  8.0 0.7 all-gather.6.cloned.1.call-update
  8.7 0.0 all-gather.4.cloned.1.call-start
  8.7 0.7 all-gather.4.cloned.1.call-update
  10.0 0.7 convert_element_type.50
  10.7 0.7 fusion.45
  11.5 0.2 reduce_window_sum.11
  11.6 0.8 select_reduce_fusion
  12.5 0.7 multiply_add_fusion
  13.1 1.5 convolution_convert_fusion.1
  14.7 1.2 reshape.51
  15.9 9.4 %all-to-all-start = ((bf16[32,5,2560]{2,1,0:T(8,128)(2,1)}), bf16[32,5,2560]{2,1,0:T(8,128)(2,1)S(1)}, u32[]{:S(2)}, u32[]{:S(2)}) async-start(bf16[32,5,2560]{2,1,0:T(8,128)(2,1)} %reshape.51), calls=%async_computation | async-start | bytes 2621440 | tf_op jit(solution)/shard_map/all_to_all | solution.py:71
  25.4 0.0 copy-done
  25.4 0.4 convolution_convert_fusion
  25.7 1.3 reshape.53
  27.1 15.6 %all-to-all-done = bf16[32,5,2560]{2,1,0:T(8,128)(2,1)S(1)} async-done(((bf16[32,5,2560]{2,1,0:T(8,128)(2,1)}), bf16[32,5,2560]{2,1,0:T(8,128)(2,1)S(1)}, u32[]{:S(2)}, u32[]{:S(2)}) %all-to-all-start) | async-done | bytes 819232 | tf_op jit(solution)/shard_map/all_to_all | solution.py:71
  42.7 7.1 %all-to-all-start.1 = ((bf16[32,5,2560]{2,1,0:T(8,128)(2,1)}), bf16[32,5,2560]{2,1,0:T(8,128)(2,1)}, u32[]{:S(2)}, u32[]{:S(2)}) async-start(bf16[32,5,2560]{2,1,0:T(8,128)(2,1)} %reshape.53), calls=%async_computation.1 | async-start | bytes 2621440 | tf_op jit(solution)/shard_map/all_to_all | solution.py:70
  49.8 0.0 reduce-scatter.2.cloned.1.call-start
  49.8 0.4 reshape.52
  50.2 16.9 %all-to-all-done.1 = bf16[32,5,2560]{2,1,0:T(8,128)(2,1)} async-done(((bf16[32,5,2560]{2,1,0:T(8,128)(2,1)}), bf16[32,5,2560]{2,1,0:T(8,128)(2,1)}, u32[]{:S(2)}, u32[]{:S(2)}) %all-to-all-start.1) | async-done | bytes 819232 | tf_op jit(solution)/shard_map/all_to_all | solution.py:70
  67.1 1.5 reshape.54
  68.6 23.4 %all-gather.8.cloned.1.call-done = bf16[1,2560,768]{2,1,0:T(8,128)(2,1)} async-done(((bf16[1,160,768]{2,1,0:T(8,128)(2,1)}), bf16[1,2560,768]{2,1,0:T(8,128)(2,1)}) %all-gather.8.cloned.1.call-update) | async-done | bytes 3932176 | tf_op jit(solution)/shard_map/all_gather | solution.py:43
  92.0 2.8 fusion.6
  94.8 73.8 %all-gather.6.cloned.1.call-done = bf16[1,2560,768]{2,1,0:T(8,128)(2,1)} async-done(((bf16[1,160,768]{2,1,0:T(8,128)(2,1)}), bf16[1,2560,768]{2,1,0:T(8,128)(2,1)}) %all-gather.6.cloned.1.call-update) | async-done | bytes 3932176 | tf_op jit(solution)/shard_map/all_gather | solution.py:44
  168.6 2.9 fusion.14
  171.5 0.0 copy-start.10
  171.6 3.1 fusion.2
  174.6 0.0 copy-done.1
  174.6 0.0 copy-start.6
  174.6 0.8 fusion.10
  175.4 0.0 copy-start.8
  175.5 0.0 copy-done.10
  175.5 0.2 copy-done.6
  175.7 1.3 fusion.36
  177.0 0.0 copy-done.8
  177.0 3.2 add_convert_fusion
  180.2 0.0 reduce-scatter.2.cloned.1.call-update
  180.2 64.9 %all-gather.4.cloned.1.call-done = bf16[1,768,2560]{2,1,0:T(8,128)(2,1)} async-done(((bf16[1,48,2560]{2,1,0:T(8,128)(2,1)}), bf16[1,768,2560]{2,1,0:T(8,128)(2,1)}) %all-gather.4.cloned.1.call-update) | async-done | bytes 3932176 | tf_op jit(solution)/shard_map/all_gather | solution.py:45
  245.1 3.7 %fusion.16 = f32[160,768]{1,0:T(8,128)S(1)} fusion(bf16[160,2560]{1,0:T(8,128)(2,1)S(1)} %reshape.52, bf16[1,768,2560]{2,1,0:T(8,128)(2,1)} %all-gather.4.cloned.1.call-done), kind=kOutput, calls=%fused_computation.17 | convolution fusion | flops 629145600 | bytes 5242880 | tf_op jit(solution)/shard_map/dot_general | solution.py:8
  248.8 0.0 copy-done.9
  248.8 0.0 copy-done.4
  248.9 0.0 copy-start.2
  248.9 1.4 fusion
  250.3 0.7 copy-done.2
  251.0 1.4 fusion.26
  252.4 0.0 copy-start.7
  252.4 1.3 reshape.55
  253.7 7.6 %all-to-all-start.2 = ((bf16[32,5,2560]{2,1,0:T(8,128)(2,1)}), bf16[32,5,2560]{2,1,0:T(8,128)(2,1)}, u32[]{:S(2)}, u32[]{:S(2)}) async-start(bf16[32,5,2560]{2,1,0:T(8,128)(2,1)} %reshape.55), calls=%async_computation.2 | async-start | bytes 2621440 | tf_op jit(solution)/shard_map/all_to_all | solution.py:76
  261.2 0.0 copy-done.7
  261.3 0.0 copy-start.5
  261.3 3.7 %fusion.18 = f32[128,768]{1,0:T(8,128)S(1)} fusion(bf16[1,768,2560]{2,1,0:T(8,128)(2,1)} %all-gather.4.cloned.1.call-done, bf16[128,2560]{1,0:T(8,128)(2,1)S(1)} %copy-done.7, f32[128]{0:T(128)S(1)} %get-tuple-element.3), kind=kOutput, calls=%fused_computation.19 | convolution fusion | flops 504299520 | bytes 4981248 | tf_op jit(solution)/shard_map/dot_general | solution.py:8
  265.0 0.0 copy-done.11
  265.0 0.0 copy-done.5
  265.0 0.0 copy-start.3
  265.0 1.4 fusion.4
  266.4 0.7 copy-done.3
  267.1 1.4 fusion.23
  268.5 10.0 %all-to-all-done.2 = bf16[32,5,2560]{2,1,0:T(8,128)(2,1)} async-done(((bf16[32,5,2560]{2,1,0:T(8,128)(2,1)}), bf16[32,5,2560]{2,1,0:T(8,128)(2,1)}, u32[]{:S(2)}, u32[]{:S(2)}) %all-to-all-start.2) | async-done | bytes 819232 | tf_op jit(solution)/shard_map/all_to_all | solution.py:76
  278.5 1.5 reshape.56
  280.0 1.2 fusion.29
  281.2 44.0 %reduce-scatter.2.cloned.1.call-done = bf16[48,2560]{1,0:T(8,128)(2,1)} async-done(((bf16[768,2560]{1,0:T(8,128)(2,1)}), bf16[48,2560]{1,0:T(8,128)(2,1)}) %reduce-scatter.2.cloned.1.call-update) | async-done | bytes 245776 | tf_op jit(solution)/shard_map/reduce_scatter | solution.py:96
  (5 shorter events, 0.0 us)
Async XLA Ops:
  7.2 18.2 %copy-start = (bf16[128,2560]{1,0:T(8,128)(2,1)S(1)}, bf16[128,2560]{1,0:T(8,128)(2,1)}, u32[]{:S(2)}) copy-start(bf16[128,2560]{1,0:T(8,128)(2,1)} %param.8) | copy-start | bytes 1966084
  7.2 84.8 %all-gather.8.cloned.1.call-start = ((), (), s32[]{:S(2)}) async-start(), calls=%async_computation.6 | async-start | bytes 4177920 | tf_op jit(solution)/shard_map/all_gather | solution.py:43
  7.9 160.7 %all-gather.6.cloned.1.call-start = ((), (), s32[]{:S(2)}) async-start(), calls=%async_computation.5 | async-start | bytes 4177920 | tf_op jit(solution)/shard_map/all_gather | solution.py:44
  8.7 236.5 %all-gather.4.cloned.1.call-start = ((), (), s32[]{:S(2)}) async-start(), calls=%async_computation.4 | async-start | bytes 4177920 | tf_op jit(solution)/shard_map/all_gather | solution.py:45
  15.9 26.7 %all-to-all-start = ((bf16[32,5,2560]{2,1,0:T(8,128)(2,1)}), bf16[32,5,2560]{2,1,0:T(8,128)(2,1)S(1)}, u32[]{:S(2)}, u32[]{:S(2)}) async-start(bf16[32,5,2560]{2,1,0:T(8,128)(2,1)} %reshape.51), calls=%async_computation | async-start | bytes 2621440 | tf_op jit(solution)/shard_map/all_to_all | solution.py:71
  42.7 24.4 %all-to-all-start.1 = ((bf16[32,5,2560]{2,1,0:T(8,128)(2,1)}), bf16[32,5,2560]{2,1,0:T(8,128)(2,1)}, u32[]{:S(2)}, u32[]{:S(2)}) async-start(bf16[32,5,2560]{2,1,0:T(8,128)(2,1)} %reshape.53), calls=%async_computation.1 | async-start | bytes 2621440 | tf_op jit(solution)/shard_map/all_to_all | solution.py:70
  49.8 275.5 %reduce-scatter.2.cloned.1.call-start = ((), (), s32[]{:S(2)}) async-start(), calls=%async_computation.7 | async-start | bytes 4177920 | tf_op jit(solution)/shard_map/reduce_scatter | solution.py:96
  168.6 6.0 %copy-start.1 = (bf16[1,2560,768]{2,1,0:T(8,128)(2,1)S(1)}, bf16[1,2560,768]{2,1,0:T(8,128)(2,1)}, u32[]{:S(2)}) copy-start(bf16[1,2560,768]{2,1,0:T(8,128)(2,1)} %all-gather.6.cloned.1.call-done) | copy-start | bytes 11796484
  171.5 3.9 %copy-start.10 = (f32[128,768]{1,0:T(8,128)}, f32[128,768]{1,0:T(8,128)S(1)}, u32[]{:S(2)}) copy-start(f32[128,768]{1,0:T(8,128)S(1)} %fusion.14) | copy-start | bytes 1179652
  174.6 1.1 copy-start.6
  175.4 1.6 copy-start.8
  180.2 68.6 %copy-start.9 = (f32[160,768]{1,0:T(8,128)S(1)}, f32[160,768]{1,0:T(8,128)}, u32[]{:S(2)}) copy-start(f32[160,768]{1,0:T(8,128)} %copy-done.8) | copy-start | bytes 1474564
  245.1 3.7 %copy-start.4 = (bf16[1,2560,768]{2,1,0:T(8,128)(2,1)S(1)}, bf16[1,2560,768]{2,1,0:T(8,128)(2,1)}, u32[]{:S(2)}) copy-start(bf16[1,2560,768]{2,1,0:T(8,128)(2,1)} %all-gather.8.cloned.1.call-done) | copy-start | bytes 11796484
  248.9 2.1 copy-start.2
  252.4 8.9 %copy-start.7 = (bf16[128,2560]{1,0:T(8,128)(2,1)S(1)}, bf16[128,2560]{1,0:T(8,128)(2,1)}, u32[]{:S(2)}) copy-start(bf16[128,2560]{1,0:T(8,128)(2,1)} %param.9) | copy-start | bytes 1966084
  253.7 11.3 %copy-start.11 = (f32[128,768]{1,0:T(8,128)S(1)}, f32[128,768]{1,0:T(8,128)}, u32[]{:S(2)}) copy-start(f32[128,768]{1,0:T(8,128)} %copy-done.10) | copy-start | bytes 1179652
  253.7 24.9 %all-to-all-start.2 = ((bf16[32,5,2560]{2,1,0:T(8,128)(2,1)}), bf16[32,5,2560]{2,1,0:T(8,128)(2,1)}, u32[]{:S(2)}, u32[]{:S(2)}) async-start(bf16[32,5,2560]{2,1,0:T(8,128)(2,1)} %reshape.55), calls=%async_computation.2 | async-start | bytes 2621440 | tf_op jit(solution)/shard_map/all_to_all | solution.py:76
  261.3 3.7 %copy-start.5 = (bf16[1,2560,768]{2,1,0:T(8,128)(2,1)S(1)}, bf16[1,2560,768]{2,1,0:T(8,128)(2,1)}, u32[]{:S(2)}) copy-start(bf16[1,2560,768]{2,1,0:T(8,128)(2,1)} %all-gather.8.cloned.1.call-done) | copy-start | bytes 11796484
  265.0 2.1 copy-start.3
Sparse Core Ops, SparseCore 0:
  10.1 81.8 all-gather.7
  94.1 74.4 all-gather.5
  170.7 74.4 all-gather.3
  248.4 76.7 reduce-scatter.1
where the time goes:
time: 333 us; the launch traced here: 332 us
  waiting for transfers between devices  251 us (75%)
  matrix products  30.2 us (9%)
  starting transfers between devices  24.2 us (7%)
  between operations  14.7 us (4%)
  local copies, waits for them, and re-layouts  8.84 us (3%)
    all_gather x1, waiting for transfers between devices, local(): lax.all_gather(w_up, 'replica', axis=1, tiled=True)  73.8 us
    all_gather x1, waiting for transfers between devices, local(): lax.all_gather(w_down, 'replica', axis=1, tiled=True)  64.9 us
    reduce_scatter x1, waiting for transfers between devices, local(): lax.psum_scatter((lax.dot_general(hidden_home, q_home, contract, preferre...  44 us
    all_gather x1, waiting for transfers between devices, local(): lax.all_gather(w_gate, 'replica', axis=1, tiled=True)  23.4 us
    all_to_all x1, waiting for transfers between devices, local(): lax.all_to_all(send_x, 'expert', split_axis=0, concat_axis=0, tiled=True)  16.9 us
    all_to_all x1, waiting for transfers between devices, local(): lax.all_to_all(send_q, 'expert', split_axis=0, concat_axis=0, tiled=True)  15.6 us
    dot_general x6, matrix products, against_rows(): lax.dot_general(left, matrix, (((1,), (1,)), ((), ())), preferred_element...  13 us
    all_to_all x1, waiting for transfers between devices, local(): lax.all_to_all(grad_there.astype(jnp.bfloat16).reshape(expert_count, item...  9.99 us
  transfers between devices with their start and end apart: 7, of which 7 were waited for; matrix products, arithmetic and copies ran while one was open for 12% of the time, Pallas kernels for 0%

commit v1 on v0

--- a/solution.py
+++ b/solution.py
@@ -2,6 +2,22 @@
 import jax.numpy as jnp
 from jax import lax
 from jax.sharding import PartitionSpec as P
+
+
+def gather_around(x, axis, dim):
+    ways, here, step = (lax.axis_size(axis), lax.axis_index(axis), x.shape[dim])
+    dims = [n * ways if d == dim else n for d, n in enumerate(x.shape)]
+    full = lax.dynamic_update_slice_in_dim(jnp.zeros(dims, x.dtype), x, here * step, axis=dim)
+    going_up = going_down = x
+    for far in range(1, ways // 2 + 1):
+        going_up = lax.ppermute(going_up, axis, [(d, (d + 1) % ways) for d in range(ways)])
+        full = lax.dynamic_update_slice_in_dim(full, going_up, (here - far) % ways * step, axis=dim)
+        if 2 * far < ways:
+            going_down = lax.ppermute(going_down, axis, [(d, (d - 1) % ways) for d in range(ways)])
+            full = lax.dynamic_update_slice_in_dim(
+                full, going_down, (here + far) % ways * step, axis=dim
+            )
+    return full
 
 
 def against_rows(left, matrix):
@@ -40,7 +56,7 @@
     q_home = (upstream * share_home[:, None]).astype(jnp.bfloat16)
     q_away = (upstream * share_away[:, None]).astype(jnp.bfloat16)
     gate_full, up_full, down_full = (
-        lax.all_gather(w_gate, "replica", axis=1, tiled=True),
+        gather_around(w_gate, "replica", 1),
         lax.all_gather(w_up, "replica", axis=1, tiled=True),
         lax.all_gather(w_down, "replica", axis=1, tiled=True),
     )

time: 333 us -> 268 us (0.80)
  the two profiles are of different devices: /device:TPU:10 before, /device:TPU:6 now
where the time goes in v1:
time: 268 us; the launch traced here: 267 us
  waiting for transfers between devices  109 us (41%)
  starting transfers between devices  80 us (30%)
  matrix products  37 us (14%)
  local copies, waits for them, and re-layouts  22.5 us (8%)
  between operations  15.1 us (6%)
  other arithmetic  3.09 us (1%)
    ppermute x7, starting transfers between devices, gather_around(): lax.ppermute(going_down, axis, [(d, (d - 1) % ways) for d in range(ways)])  40.3 us
    reduce_scatter x1, waiting for transfers between devices, local(): lax.psum_scatter((lax.dot_general(hidden_home, q_home, contract, preferre...  36.4 us
    ppermute x8, waiting for transfers between devices, gather_around(): lax.ppermute(going_up, axis, [(d, (d + 1) % ways) for d in range(ways)])  26.9 us
    all_gather x1, waiting for transfers between devices, local(): lax.all_gather(w_down, 'replica', axis=1, tiled=True)  24.9 us
    dot_general x6, matrix products, against_rows(): lax.dot_general(left, matrix, (((1,), (1,)), ((), ())), preferred_element...  19.6 us
    ppermute x8, starting transfers between devices, gather_around(): lax.ppermute(going_up, axis, [(d, (d + 1) % ways) for d in range(ways)])  17.4 us
    all_to_all x1, waiting for transfers between devices, local(): lax.all_to_all(grad_there.astype(jnp.bfloat16).reshape(expert_count, item...  11.2 us
    all_to_all x1, waiting for transfers between devices, local(): lax.all_to_all(send_x, 'expert', split_axis=0, concat_axis=0, tiled=True)  7.77 us
  transfers between devices with their start and end apart: 21, of which 10 were waited for; matrix products, arithmetic and copies ran while one was open for 23% of the time, Pallas kernels for 0%

profile of v1, /device:TPU:6, one launch (start us, length us, event | category | flops | bytes accessed | tf_op | source)
XLA Modules:
  0.0 266.6 jit_solution(12055366261940696526)
XLA Ops:
  8.0 3.8 %collective-permute-start = (bf16[1,160,768]{2,1,0:T(8,128)(2,1)}, bf16[1,160,768]{2,1,0:T(8,128)(2,1)S(1)}, u32[]{:S(2)}, u32[]{:S(2)}) collective-permute-start(bf16[1,160,768]{2,1,0:T(8,128)(2,1)} %param.13), channel_id=1, source_target_pairs={{0,1},{1,2},{2,3},{3,4},{4,5},{5,6},{6,7},{7,8},{8,9},{9,10},{10,1... | collective-permute-start | bytes 737288 | tf_op jit(solution)/shard_map/ppermute | solution.py:13
  11.8 9.5 %collective-permute-start.1 = (bf16[1,160,768]{2,1,0:T(8,128)(2,1)}, bf16[1,160,768]{2,1,0:T(8,128)(2,1)S(1)}, u32[]{:S(2)}, u32[]{:S(2)}) collective-permute-start(bf16[1,160,768]{2,1,0:T(8,128)(2,1)} %param.13), channel_id=1, source_target_pairs={{0,15},{1,0},{2,1},{3,2},{4,3},{5,4},{6,5},{7,6},{8,7},{9,8},{10,9... | collective-permute-start | bytes 737288 | tf_op jit(solution)/shard_map/ppermute | solution.py:16
  21.3 0.7 fusion.31
  23.6 0.8 select_reduce_fusion
  25.1 1.5 convolution_convert_fusion.1
  26.6 1.3 reshape.131
  27.9 7.6 %all-to-all-start = ((bf16[32,5,2560]{2,1,0:T(8,128)(2,1)}), bf16[32,5,2560]{2,1,0:T(8,128)(2,1)S(1)}, u32[]{:S(2)}, u32[]{:S(2)}) async-start(bf16[32,5,2560]{2,1,0:T(8,128)(2,1)} %reshape.131), calls=%async_computation | async-start | bytes 2621440 | tf_op jit(solution)/shard_map/all_to_all | solution.py:87
  36.2 1.3 reshape.133
  37.5 2.1 reshape.114
  40.3 1.9 collective-permute-start.2
  42.3 5.1 %collective-permute-start.3 = (bf16[1,160,768]{2,1,0:T(8,128)(2,1)S(1)}, bf16[1,160,768]{2,1,0:T(8,128)(2,1)S(1)}, u32[]{:S(2)}, u32[]{:S(2)}) collective-permute-start(bf16[1,160,768]{2,1,0:T(8,128)(2,1)S(1)} %collective-permute-done.1), channel_id=1, source_target_pairs={{0,15},{1,0},{2,1},{3,2},{4,3},{5,4},{6,5},{7,6},{8,7},{9,8},{10,9... | collective-permute-start | bytes 737288 | tf_op jit(solution)/shard_map/ppermute | solution.py:16
  48.1 0.7 bitcast_dynamic-update-slice_fusion.13
  48.8 7.4 %collective-permute-done.2 = bf16[1,160,768]{2,1,0:T(8,128)(2,1)S(1)} collective-permute-done((bf16[1,160,768]{2,1,0:T(8,128)(2,1)S(1)}, bf16[1,160,768]{2,1,0:T(8,128)(2,1)S(1)}, u32[]{:S(2)}, u32[]{:S(2)}) %collective-permute-start.2) | collective-permute-done | bytes 245792 | tf_op jit(solution)/shard_map/ppermute | solution.py:13
  56.2 1.9 collective-permute-start.4
  58.1 5.1 %collective-permute-start.5 = (bf16[1,160,768]{2,1,0:T(8,128)(2,1)S(1)}, bf16[1,160,768]{2,1,0:T(8,128)(2,1)S(1)}, u32[]{:S(2)}, u32[]{:S(2)}) collective-permute-start(bf16[1,160,768]{2,1,0:T(8,128)(2,1)S(1)} %collective-permute-done.3), channel_id=1, source_target_pairs={{0,15},{1,0},{2,1},{3,2},{4,3},{5,4},{6,5},{7,6},{8,7},{9,8},{10,9... | collective-permute-start | bytes 737288 | tf_op jit(solution)/shard_map/ppermute | solution.py:16
  63.2 7.3 %all-to-all-start.1 = ((bf16[32,5,2560]{2,1,0:T(8,128)(2,1)}), bf16[32,5,2560]{2,1,0:T(8,128)(2,1)}, u32[]{:S(2)}, u32[]{:S(2)}) async-start(bf16[32,5,2560]{2,1,0:T(8,128)(2,1)} %reshape.133), calls=%async_computation.1 | async-start | bytes 2621440 | tf_op jit(solution)/shard_map/all_to_all | solution.py:86
  70.6 0.7 bitcast_dynamic-update-slice_fusion.12
  71.3 0.7 bitcast_dynamic-update-slice_fusion.11
  72.0 1.9 collective-permute-start.6
  73.9 5.1 %collective-permute-start.7 = (bf16[1,160,768]{2,1,0:T(8,128)(2,1)S(1)}, bf16[1,160,768]{2,1,0:T(8,128)(2,1)}, u32[]{:S(2)}, u32[]{:S(2)}) collective-permute-start(bf16[1,160,768]{2,1,0:T(8,128)(2,1)S(1)} %collective-permute-done.5), channel_id=1, source_target_pairs={{0,15},{1,0},{2,1},{3,2},{4,3},{5,4},{6,5},{7,6},{8,7},{9,8},{10,9... | collective-permute-start | bytes 737288 | tf_op jit(solution)/shard_map/ppermute | solution.py:16
  79.1 0.7 bitcast_dynamic-update-slice_fusion.10
  79.8 0.7 bitcast_dynamic-update-slice_fusion.9
  80.9 7.8 %all-to-all-done.1 = bf16[32,5,2560]{2,1,0:T(8,128)(2,1)} async-done(((bf16[32,5,2560]{2,1,0:T(8,128)(2,1)}), bf16[32,5,2560]{2,1,0:T(8,128)(2,1)}, u32[]{:S(2)}, u32[]{:S(2)}) %all-to-all-start.1) | async-done | bytes 819232 | tf_op jit(solution)/shard_map/all_to_all | solution.py:86
  88.7 1.5 reshape.134
  90.2 1.9 collective-permute-start.8
  92.1 5.1 %collective-permute-start.9 = (bf16[1,160,768]{2,1,0:T(8,128)(2,1)}, bf16[1,160,768]{2,1,0:T(8,128)(2,1)S(1)}, u32[]{:S(2)}, u32[]{:S(2)}) collective-permute-start(bf16[1,160,768]{2,1,0:T(8,128)(2,1)} %collective-permute-done.7), channel_id=1, source_target_pairs={{0,15},{1,0},{2,1},{3,2},{4,3},{5,4},{6,5},{7,6},{8,7},{9,8},{10,9... | collective-permute-start | bytes 737288 | tf_op jit(solution)/shard_map/ppermute | solution.py:16
  97.3 0.7 bitcast_dynamic-update-slice_fusion.8
  98.0 1.7 bitcast_dynamic-update-slice_fusion.7
  99.7 3.3 %collective-permute-done.8 = bf16[1,160,768]{2,1,0:T(8,128)(2,1)S(1)} collective-permute-done((bf16[1,160,768]{2,1,0:T(8,128)(2,1)S(1)}, bf16[1,160,768]{2,1,0:T(8,128)(2,1)S(1)}, u32[]{:S(2)}, u32[]{:S(2)}) %collective-permute-start.8) | collective-permute-done | bytes 245792 | tf_op jit(solution)/shard_map/ppermute | solution.py:13
  102.9 1.9 collective-permute-start.10
  104.8 5.1 %collective-permute-start.11 = (bf16[1,160,768]{2,1,0:T(8,128)(2,1)S(1)}, bf16[1,160,768]{2,1,0:T(8,128)(2,1)S(1)}, u32[]{:S(2)}, u32[]{:S(2)}) collective-permute-start(bf16[1,160,768]{2,1,0:T(8,128)(2,1)S(1)} %collective-permute-done.9), channel_id=1, source_target_pairs={{0,15},{1,0},{2,1},{3,2},{4,3},{5,4},{6,5},{7,6},{8,7},{9,8},{10,9... | collective-permute-start | bytes 737288 | tf_op jit(solution)/shard_map/ppermute | solution.py:16
  110.0 0.7 bitcast_dynamic-update-slice_fusion.6
  110.7 0.7 bitcast_dynamic-update-slice_fusion.5
  111.4 2.0 collective-permute-done.10
  113.4 1.9 collective-permute-start.12
  115.3 5.1 %collective-permute-start.13 = (bf16[1,160,768]{2,1,0:T(8,128)(2,1)S(1)}, bf16[1,160,768]{2,1,0:T(8,128)(2,1)S(1)}, u32[]{:S(2)}, u32[]{:S(2)}) collective-permute-start(bf16[1,160,768]{2,1,0:T(8,128)(2,1)S(1)} %collective-permute-done.11), channel_id=1, source_target_pairs={{0,15},{1,0},{2,1},{3,2},{4,3},{5,4},{6,5},{7,6},{8,7},{9,8},{10,9... | collective-permute-start | bytes 737288 | tf_op jit(solution)/shard_map/ppermute | solution.py:16
  120.5 0.7 bitcast_dynamic-update-slice_fusion.4
  121.9 4.2 %collective-permute-done.12 = bf16[1,160,768]{2,1,0:T(8,128)(2,1)S(1)} collective-permute-done((bf16[1,160,768]{2,1,0:T(8,128)(2,1)S(1)}, bf16[1,160,768]{2,1,0:T(8,128)(2,1)S(1)}, u32[]{:S(2)}, u32[]{:S(2)}) %collective-permute-start.12) | collective-permute-done | bytes 245792 | tf_op jit(solution)/shard_map/ppermute | solution.py:13
  126.1 2.1 collective-permute-start.14
  128.2 0.7 bitcast_dynamic-update-slice_fusion.2
  128.9 0.9 collective-permute-done.13
  129.8 0.7 bitcast_dynamic-update-slice_fusion.1
  130.5 10.1 %collective-permute-done.14 = bf16[1,160,768]{2,1,0:T(8,128)(2,1)S(1)} collective-permute-done((bf16[1,160,768]{2,1,0:T(8,128)(2,1)S(1)}, bf16[1,160,768]{2,1,0:T(8,128)(2,1)S(1)}, u32[]{:S(2)}, u32[]{:S(2)}) %collective-permute-start.14) | collective-permute-done | bytes 245792 | tf_op jit(solution)/shard_map/ppermute | solution.py:13
  140.7 0.7 bitcast_dynamic-update-slice_fusion
  141.4 2.8 %convolution_bitcast_fusion = f32[128,768]{1,0:T(8,128)S(1)} fusion(bf16[128,2560]{1,0:T(8,128)(2,1)S(1)} %copy-done, bf16[2560,768]{1,0:T(8,128)(2,1)} %bitcast_dynamic-update-slice_fusion), kind=kOutput, calls=%fused_computation.24 | convolution fusion | flops 503316480 | bytes 4980736 | tf_op jit(solution)/shard_map/dot_general | solution.py:30
  144.2 2.9 %fusion.43 = f32[160,768]{1,0:T(8,128)S(1)} fusion(bf16[160,2560]{1,0:T(8,128)(2,1)S(1)} %reshape.134, bf16[2560,768]{1,0:T(8,128)(2,1)} %bitcast_dynamic-update-slice_fusion), kind=kOutput, calls=%fused_computation.76 | convolution fusion | flops 629145600 | bytes 5242880 | tf_op jit(solution)/shard_map/dot_general | solution.py:30
  147.2 3.0 %fusion.6 = f32[128,768]{1,0:T(8,128)S(1)} fusion(bf16[128,2560]{1,0:T(8,128)(2,1)S(1)} %copy-done, bf16[1,2560,768]{2,1,0:T(8,128)(2,1)} %all-gather.5.cloned.1.call-done), kind=kOutput, calls=%fused_computation.7 | convolution fusion | flops 503316480 | bytes 4980736 | tf_op jit(solution)/shard_map/dot_general | solution.py:31
  150.5 0.8 fusion.2
  151.4 1.3 fusion.21
  152.7 3.2 %add_convert_fusion = bf16[768,2560]{1,0:T(8,128)(2,1)} fusion(f32[768,2560]{1,0:T(8,128)S(1)} %fusion.21, bf16[160,2560]{1,0:T(8,128)(2,1)S(1)} %reshape.132, f32[160,768]{1,0:T(8,128)S(1)} %fusion.2, f32[160,768]{1,0:T(8,128)S(1)} %fusion.43), kind=kOutput, calls=%fused_computation | convolution fusion | flops 633815040 | bytes 13598720 | tf_op jit(solution)/shard_map/dot_general | solution.py:115
  155.8 24.9 %all-gather.3.cloned.1.call-done = bf16[1,768,2560]{2,1,0:T(8,128)(2,1)} async-done(((bf16[1,48,2560]{2,1,0:T(8,128)(2,1)}), bf16[1,768,2560]{2,1,0:T(8,128)(2,1)}) %all-gather.3.cloned.1.call-update) | async-done | bytes 3932176 | tf_op jit(solution)/shard_map/all_gather | solution.py:61
  180.7 3.7 %fusion.8 = f32[160,768]{1,0:T(8,128)S(1)} fusion(bf16[160,2560]{1,0:T(8,128)(2,1)S(1)} %reshape.132, bf16[1,768,2560]{2,1,0:T(8,128)(2,1)} %all-gather.3.cloned.1.call-done), kind=kOutput, calls=%fused_computation.9 | convolution fusion | flops 629145600 | bytes 5242880 | tf_op jit(solution)/shard_map/dot_general | solution.py:24
  184.4 1.4 fusion
  185.8 3.6 %fusion.13 = bf16[160,2560]{1,0:T(8,128)(2,1)S(1)} fusion(f32[160,2560]{1,0:T(8,128)S(1)} %fusion, bf16[2560,768]{1,0:T(8,128)(2,1)} %bitcast_dynamic-update-slice_fusion, f32[160,768]{1,0:T(8,128)S(1)} %fusion.43, f32[160,768]{1,0:T(8,128)S(1)} %fusion.8, f32[160,768]{1,0:T(8,128)S(1)} %copy-done.7), kind=kOutput, calls=%fused_computation.16 | convolution fusion | flops 631193600 | bytes 7864320 | tf_op jit(solution)/shard_map/dot_general | solution.py:24
  189.4 1.2 reshape.135
  190.7 7.4 %all-to-all-start.2 = ((bf16[32,5,2560]{2,1,0:T(8,128)(2,1)}), bf16[32,5,2560]{2,1,0:T(8,128)(2,1)S(1)}, u32[]{:S(2)}, u32[]{:S(2)}) async-start(bf16[32,5,2560]{2,1,0:T(8,128)(2,1)} %reshape.135), calls=%async_computation.2 | async-start | bytes 2621440 | tf_op jit(solution)/shard_map/all_to_all | solution.py:92
  198.1 3.7 %fusion.10 = f32[128,768]{1,0:T(8,128)S(1)} fusion(bf16[1,768,2560]{2,1,0:T(8,128)(2,1)} %all-gather.3.cloned.1.call-done, bf16[128,2560]{1,0:T(8,128)(2,1)S(1)} %copy-done.5, f32[128]{0:T(128)S(1)} %get-tuple-element.2), kind=kOutput, calls=%fused_computation.11 | convolution fusion | flops 504299520 | bytes 4981248 | tf_op jit(solution)/shard_map/dot_general | solution.py:24
  201.8 0.7 copy-done.10
  202.5 2.5 fusion.4
  205.0 11.2 %all-to-all-done.2 = bf16[32,5,2560]{2,1,0:T(8,128)(2,1)S(1)} async-done(((bf16[32,5,2560]{2,1,0:T(8,128)(2,1)}), bf16[32,5,2560]{2,1,0:T(8,128)(2,1)S(1)}, u32[]{:S(2)}, u32[]{:S(2)}) %all-to-all-start.2) | async-done | bytes 819232 | tf_op jit(solution)/shard_map/all_to_all | solution.py:92
  216.2 1.1 reshape.136
  217.3 1.5 fusion.28
  218.8 4.8 %fusion.14 = bf16[128,2560]{1,0:T(8,128)(2,1)} fusion(f32[128,2560]{1,0:T(8,128)S(1)} %fusion.28, f32[128,2560]{1,0:T(8,128)} %fusion.4, bf16[2560,768]{1,0:T(8,128)(2,1)} %bitcast_dynamic-update-slice_fusion, f32[128,768]{1,0:T(8,128)S(1)} %convolution_bitcast_fusion, f32[128,768]{1,0:T(8,128)S(1)} %copy-done.11, f32[128,768]{1,0:T(8,128)S(1)} %copy-done.9), kind=kOutput, calls=%fused_computation.19 | convolution fusion | flops 505282560 | bytes 8388608 | tf_op jit(solution)/shard_map/dot_general | solution.py:24
  223.7 36.4 %reduce-scatter.2.cloned.1.call-done = bf16[48,2560]{1,0:T(8,128)(2,1)} async-done(((bf16[768,2560]{1,0:T(8,128)(2,1)}), bf16[48,2560]{1,0:T(8,128)(2,1)}) %reduce-scatter.2.cloned.1.call-update) | async-done | bytes 245776 | tf_op jit(solution)/shard_map/reduce_scatter | solution.py:112
  (51 shorter events, 5.7 us)
Async XLA Ops:
  7.2 28.4 %copy-start = (bf16[128,2560]{1,0:T(8,128)(2,1)S(1)}, bf16[128,2560]{1,0:T(8,128)(2,1)}, u32[]{:S(2)}) copy-start(bf16[128,2560]{1,0:T(8,128)(2,1)} %param.8) | copy-start | bytes 1966084
  7.2 140.0 %all-gather.5.cloned.1.call-start = ((), (), s32[]{:S(2)}) async-start(), calls=%async_computation.5 | async-start | bytes 4177920 | tf_op jit(solution)/shard_map/all_gather | solution.py:60
  7.9 172.8 %all-gather.3.cloned.1.call-start = ((), (), s32[]{:S(2)}) async-start(), calls=%async_computation.4 | async-start | bytes 4177920 | tf_op jit(solution)/shard_map/all_gather | solution.py:61
  8.0 32.4 %collective-permute-start = (bf16[1,160,768]{2,1,0:T(8,128)(2,1)}, bf16[1,160,768]{2,1,0:T(8,128)(2,1)S(1)}, u32[]{:S(2)}, u32[]{:S(2)}) collective-permute-start(bf16[1,160,768]{2,1,0:T(8,128)(2,1)} %param.13), channel_id=1, source_target_pairs={{0,1},{1,2},{2,3},{3,4},{4,5},{5,6},{6,7},{7,8},{8,9},{9,10},{10,1... | collective-permute-start | bytes 737288 | tf_op jit(solution)/shard_map/ppermute | solution.py:13
  11.8 30.5 %collective-permute-start.1 = (bf16[1,160,768]{2,1,0:T(8,128)(2,1)}, bf16[1,160,768]{2,1,0:T(8,128)(2,1)S(1)}, u32[]{:S(2)}, u32[]{:S(2)}) collective-permute-start(bf16[1,160,768]{2,1,0:T(8,128)(2,1)} %param.13), channel_id=1, source_target_pairs={{0,15},{1,0},{2,1},{3,2},{4,3},{5,4},{6,5},{7,6},{8,7},{9,8},{10,9... | collective-permute-start | bytes 737288 | tf_op jit(solution)/shard_map/ppermute | solution.py:16
  27.9 35.3 %all-to-all-start = ((bf16[32,5,2560]{2,1,0:T(8,128)(2,1)}), bf16[32,5,2560]{2,1,0:T(8,128)(2,1)S(1)}, u32[]{:S(2)}, u32[]{:S(2)}) async-start(bf16[32,5,2560]{2,1,0:T(8,128)(2,1)} %reshape.131), calls=%async_computation | async-start | bytes 2621440 | tf_op jit(solution)/shard_map/all_to_all | solution.py:87
  35.5 4.1 %copy-start.12 = (bf16[1,160,768]{2,1,0:T(8,128)(2,1)S(1)}, bf16[1,160,768]{2,1,0:T(8,128)(2,1)}, u32[]{:S(2)}) copy-start(bf16[1,160,768]{2,1,0:T(8,128)(2,1)} %param.13) | copy-start | bytes 737284
  40.3 15.8 %collective-permute-start.2 = (bf16[1,160,768]{2,1,0:T(8,128)(2,1)S(1)}, bf16[1,160,768]{2,1,0:T(8,128)(2,1)S(1)}, u32[]{:S(2)}, u32[]{:S(2)}) collective-permute-start(bf16[1,160,768]{2,1,0:T(8,128)(2,1)S(1)} %collective-permute-done), channel_id=1, source_target_pairs={{0,1},{1,2},{2,3},{3,4},{4,5},{5,6},{6,7},{7,8},{8,9},{9,10},{10,1... | collective-permute-start | bytes 737288 | tf_op jit(solution)/shard_map/ppermute | solution.py:13
  42.3 15.8 %collective-permute-start.3 = (bf16[1,160,768]{2,1,0:T(8,128)(2,1)S(1)}, bf16[1,160,768]{2,1,0:T(8,128)(2,1)S(1)}, u32[]{:S(2)}, u32[]{:S(2)}) collective-permute-start(bf16[1,160,768]{2,1,0:T(8,128)(2,1)S(1)} %collective-permute-done.1), channel_id=1, source_target_pairs={{0,15},{1,0},{2,1},{3,2},{4,3},{5,4},{6,5},{7,6},{8,7},{9,8},{10,9... | collective-permute-start | bytes 737288 | tf_op jit(solution)/shard_map/ppermute | solution.py:16
  56.2 15.8 %collective-permute-start.4 = (bf16[1,160,768]{2,1,0:T(8,128)(2,1)S(1)}, bf16[1,160,768]{2,1,0:T(8,128)(2,1)S(1)}, u32[]{:S(2)}, u32[]{:S(2)}) collective-permute-start(bf16[1,160,768]{2,1,0:T(8,128)(2,1)S(1)} %collective-permute-done.2), channel_id=1, source_target_pairs={{0,1},{1,2},{2,3},{3,4},{4,5},{5,6},{6,7},{7,8},{8,9},{9,10},{10,1... | collective-permute-start | bytes 737288 | tf_op jit(solution)/shard_map/ppermute | solution.py:13
  58.1 15.8 %collective-permute-start.5 = (bf16[1,160,768]{2,1,0:T(8,128)(2,1)S(1)}, bf16[1,160,768]{2,1,0:T(8,128)(2,1)S(1)}, u32[]{:S(2)}, u32[]{:S(2)}) collective-permute-start(bf16[1,160,768]{2,1,0:T(8,128)(2,1)S(1)} %collective-permute-done.3), channel_id=1, source_target_pairs={{0,15},{1,0},{2,1},{3,2},{4,3},{5,4},{6,5},{7,6},{8,7},{9,8},{10,9... | collective-permute-start | bytes 737288 | tf_op jit(solution)/shard_map/ppermute | solution.py:16
  63.2 25.4 %all-to-all-start.1 = ((bf16[32,5,2560]{2,1,0:T(8,128)(2,1)}), bf16[32,5,2560]{2,1,0:T(8,128)(2,1)}, u32[]{:S(2)}, u32[]{:S(2)}) async-start(bf16[32,5,2560]{2,1,0:T(8,128)(2,1)} %reshape.133), calls=%async_computation.1 | async-start | bytes 2621440 | tf_op jit(solution)/shard_map/all_to_all | solution.py:86
  70.5 189.5 %reduce-scatter.2.cloned.1.call-start = ((), (), s32[]{:S(2)}) async-start(), calls=%async_computation.6 | async-start | bytes 4177920 | tf_op jit(solution)/shard_map/reduce_scatter | solution.py:112
  72.0 18.2 %collective-permute-start.6 = (bf16[1,160,768]{2,1,0:T(8,128)(2,1)S(1)}, bf16[1,160,768]{2,1,0:T(8,128)(2,1)S(1)}, u32[]{:S(2)}, u32[]{:S(2)}) collective-permute-start(bf16[1,160,768]{2,1,0:T(8,128)(2,1)S(1)} %collective-permute-done.4), channel_id=1, source_target_pairs={{0,1},{1,2},{2,3},{3,4},{4,5},{5,6},{6,7},{7,8},{8,9},{9,10},{10,1... | collective-permute-start | bytes 737288 | tf_op jit(solution)/shard_map/ppermute | solution.py:13
  73.9 18.2 %collective-permute-start.7 = (bf16[1,160,768]{2,1,0:T(8,128)(2,1)S(1)}, bf16[1,160,768]{2,1,0:T(8,128)(2,1)}, u32[]{:S(2)}, u32[]{:S(2)}) collective-permute-start(bf16[1,160,768]{2,1,0:T(8,128)(2,1)S(1)} %collective-permute-done.5), channel_id=1, source_target_pairs={{0,15},{1,0},{2,1},{3,2},{4,3},{5,4},{6,5},{7,6},{8,7},{9,8},{10,9... | collective-permute-start | bytes 737288 | tf_op jit(solution)/shard_map/ppermute | solution.py:16
  90.2 12.7 %collective-permute-start.8 = (bf16[1,160,768]{2,1,0:T(8,128)(2,1)S(1)}, bf16[1,160,768]{2,1,0:T(8,128)(2,1)S(1)}, u32[]{:S(2)}, u32[]{:S(2)}) collective-permute-start(bf16[1,160,768]{2,1,0:T(8,128)(2,1)S(1)} %collective-permute-done.6), channel_id=1, source_target_pairs={{0,1},{1,2},{2,3},{3,4},{4,5},{5,6},{6,7},{7,8},{8,9},{9,10},{10,1... | collective-permute-start | bytes 737288 | tf_op jit(solution)/shard_map/ppermute | solution.py:13
  92.1 12.7 %collective-permute-start.9 = (bf16[1,160,768]{2,1,0:T(8,128)(2,1)}, bf16[1,160,768]{2,1,0:T(8,128)(2,1)S(1)}, u32[]{:S(2)}, u32[]{:S(2)}) collective-permute-start(bf16[1,160,768]{2,1,0:T(8,128)(2,1)} %collective-permute-done.7), channel_id=1, source_target_pairs={{0,15},{1,0},{2,1},{3,2},{4,3},{5,4},{6,5},{7,6},{8,7},{9,8},{10,9... | collective-permute-start | bytes 737288 | tf_op jit(solution)/shard_map/ppermute | solution.py:16
  102.9 10.5 %collective-permute-start.10 = (bf16[1,160,768]{2,1,0:T(8,128)(2,1)S(1)}, bf16[1,160,768]{2,1,0:T(8,128)(2,1)S(1)}, u32[]{:S(2)}, u32[]{:S(2)}) collective-permute-start(bf16[1,160,768]{2,1,0:T(8,128)(2,1)S(1)} %collective-permute-done.8), channel_id=1, source_target_pairs={{0,1},{1,2},{2,3},{3,4},{4,5},{5,6},{6,7},{7,8},{8,9},{9,10},{10,1... | collective-permute-start | bytes 737288 | tf_op jit(solution)/shard_map/ppermute | solution.py:13
  104.8 10.5 %collective-permute-start.11 = (bf16[1,160,768]{2,1,0:T(8,128)(2,1)S(1)}, bf16[1,160,768]{2,1,0:T(8,128)(2,1)S(1)}, u32[]{:S(2)}, u32[]{:S(2)}) collective-permute-start(bf16[1,160,768]{2,1,0:T(8,128)(2,1)S(1)} %collective-permute-done.9), channel_id=1, source_target_pairs={{0,15},{1,0},{2,1},{3,2},{4,3},{5,4},{6,5},{7,6},{8,7},{9,8},{10,9... | collective-permute-start | bytes 737288 | tf_op jit(solution)/shard_map/ppermute | solution.py:16
  113.4 12.7 %collective-permute-start.12 = (bf16[1,160,768]{2,1,0:T(8,128)(2,1)S(1)}, bf16[1,160,768]{2,1,0:T(8,128)(2,1)S(1)}, u32[]{:S(2)}, u32[]{:S(2)}) collective-permute-start(bf16[1,160,768]{2,1,0:T(8,128)(2,1)S(1)} %collective-permute-done.10), channel_id=1, source_target_pairs={{0,1},{1,2},{2,3},{3,4},{4,5},{5,6},{6,7},{7,8},{8,9},{9,10},{10,1... | collective-permute-start | bytes 737288 | tf_op jit(solution)/shard_map/ppermute | solution.py:13
  115.3 14.5 %collective-permute-start.13 = (bf16[1,160,768]{2,1,0:T(8,128)(2,1)S(1)}, bf16[1,160,768]{2,1,0:T(8,128)(2,1)S(1)}, u32[]{:S(2)}, u32[]{:S(2)}) collective-permute-start(bf16[1,160,768]{2,1,0:T(8,128)(2,1)S(1)} %collective-permute-done.11), channel_id=1, source_target_pairs={{0,15},{1,0},{2,1},{3,2},{4,3},{5,4},{6,5},{7,6},{8,7},{9,8},{10,9... | collective-permute-start | bytes 737288 | tf_op jit(solution)/shard_map/ppermute | solution.py:16
  126.1 14.6 %collective-permute-start.14 = (bf16[1,160,768]{2,1,0:T(8,128)(2,1)S(1)}, bf16[1,160,768]{2,1,0:T(8,128)(2,1)S(1)}, u32[]{:S(2)}, u32[]{:S(2)}) collective-permute-start(bf16[1,160,768]{2,1,0:T(8,128)(2,1)S(1)} %collective-permute-done.12), channel_id=1, source_target_pairs={{0,1},{1,2},{2,3},{3,4},{4,5},{5,6},{6,7},{7,8},{8,9},{9,10},{10,1... | collective-permute-start | bytes 737288 | tf_op jit(solution)/shard_map/ppermute | solution.py:13
  147.2 3.3 %copy-start.1 = (bf16[1,2560,768]{2,1,0:T(8,128)(2,1)S(1)}, bf16[1,2560,768]{2,1,0:T(8,128)(2,1)}, u32[]{:S(2)}) copy-start(bf16[1,2560,768]{2,1,0:T(8,128)(2,1)} %all-gather.5.cloned.1.call-done) | copy-start | bytes 11796484
  147.2 4.2 %copy-start.4 = (bf16[128,2560]{1,0:T(8,128)(2,1)S(1)}, bf16[128,2560]{1,0:T(8,128)(2,1)}, u32[]{:S(2)}) copy-start(bf16[128,2560]{1,0:T(8,128)(2,1)} %param.9) | copy-start | bytes 1966084
  150.5 0.8 copy-start.8
  151.3 1.3 copy-start.6
  180.7 3.7 %copy-start.2 = (bf16[1,2560,768]{2,1,0:T(8,128)(2,1)S(1)}, bf16[1,2560,768]{2,1,0:T(8,128)(2,1)}, u32[]{:S(2)}) copy-start(bf16[1,2560,768]{2,1,0:T(8,128)(2,1)} %all-gather.5.cloned.1.call-done) | copy-start | bytes 11796484
  184.4 1.5 copy-start.7
  189.4 8.7 %copy-start.5 = (bf16[128,2560]{1,0:T(8,128)(2,1)S(1)}, bf16[128,2560]{1,0:T(8,128)(2,1)}, u32[]{:S(2)}) copy-start(bf16[128,2560]{1,0:T(8,128)(2,1)} %param.9) | copy-start | bytes 1966084
  190.7 25.5 %all-to-all-start.2 = ((bf16[32,5,2560]{2,1,0:T(8,128)(2,1)}), bf16[32,5,2560]{2,1,0:T(8,128)(2,1)S(1)}, u32[]{:S(2)}, u32[]{:S(2)}) async-start(bf16[32,5,2560]{2,1,0:T(8,128)(2,1)} %reshape.135), calls=%async_computation.2 | async-start | bytes 2621440 | tf_op jit(solution)/shard_map/all_to_all | solution.py:92
  198.1 4.4 %copy-start.3 = (bf16[1,2560,768]{2,1,0:T(8,128)(2,1)S(1)}, bf16[1,2560,768]{2,1,0:T(8,128)(2,1)}, u32[]{:S(2)}) copy-start(bf16[1,2560,768]{2,1,0:T(8,128)(2,1)} %all-gather.5.cloned.1.call-done) | copy-start | bytes 11796484
  201.8 0.7 copy-start.10
  202.5 16.3 %copy-start.9 = (f32[128,768]{1,0:T(8,128)S(1)}, f32[128,768]{1,0:T(8,128)}, u32[]{:S(2)}) copy-start(f32[128,768]{1,0:T(8,128)} %copy-done.8) | copy-start | bytes 1179652
  205.0 13.8 %copy-start.11 = (f32[128,768]{1,0:T(8,128)S(1)}, f32[128,768]{1,0:T(8,128)}, u32[]{:S(2)}) copy-start(f32[128,768]{1,0:T(8,128)} %copy-done.10) | copy-start | bytes 1179652
Sparse Core Ops, SparseCore 0:
  10.1 92.6 all-gather.4
  104.8 75.8 all-gather.2
  184.1 75.8 reduce-scatter.1
